TPU v7x, 128 devices: a whole 4x4x4 slice. The times are simulated.
128 devices in a mesh: tok: 16 (over y, z), own: 8 (over x, core).
Axes of the slice: x: 4, y: 4, z: 4, core: 2. Of those that a mesh axis runs over, the one named last changes fastest.
Arguments:
- tokens: bfloat16 [16384, 1152], P(('tok', 'own')), may hold values from -6 to 6
- norm_gain: bfloat16 [1152], replicated, may hold values from 0.099609375 to 1.8984375
- w_query: bfloat16 [1152, 1152], replicated, as said below
- w_key: bfloat16 [1152, 384], replicated, as said below
- w_value: bfloat16 [1152, 384], replicated, may hold values from -0.1875 to 0.1875
- w_output: bfloat16 [1152, 1152], replicated, may hold values from -0.1875 to 0.1875
- qkv_in: bfloat16 [64, 48, 1152], P('own', None, 'tok'), may hold values from -0.1875 to 0.1875
- q_out: bfloat16 [64, 16, 1152], P('own', None, 'tok'), may hold values from -1.5 to 1.5
- kv_out: bfloat16 [64, 32, 384], P('own', None, 'tok'), may hold values from -1.5 to 1.5
- o_in: bfloat16 [64, 16, 1152], P('own', None, 'tok'), may hold values from -0.1875 to 0.1875
- o_out: bfloat16 [64, 16, 1152], P('own', None, 'tok'), may hold values from -1.5 to 1.5
- lengths: int32 [64], replicated, may hold values from 32 to 1536, as said below
- prompt_adapter: int32 [64], replicated, may hold values from 0 to 63
- adapter_slot: int32 [64], replicated, may hold values from 0 to 63, each once
Outputs:
- mixed: bfloat16 [16384, 1152], P(('tok', 'own'))
- kv_cache: bfloat16 [16384, 768], P(('tok', 'own'))
Inputs may be any that keep to these rules, and one draw needn't show every extreme that they name: `w_query`: entries lie within 6 / sqrt(1152) of zero. `w_key`: entries lie within 6 / sqrt(1152) of zero. `lengths`: lengths sum to 16384; exactly 8 prompts are 1536 long; the others hold 32 to 128 tokens, and one of them exactly 32. `adapter_slot`: each slot appears once; slot s is row s of the adapter tables, held by own index s // 8.
All inputs are finite; a program needn't handle non-finite values.
Results may differ from a plain program's by a relative error of at most 0.02.
Values may be sent and summed in bfloat16 or wider, within the bound.
No kernel may reach another device: no remote copies, remote signals or barrier semaphores. Data moves between devices by JAX's collectives and lax.ppermute only.
A program may use at most 128 MiB of HBM per device.

v0:
```python
import math
import jax
import jax.numpy as jnp
from jax import lax
from jax.sharding import PartitionSpec as P

D = 1152
HEADS = 18
KV_HEADS = 6
HEAD_WIDTH = 64
RANK = 16
REACH = 12
KVW = 384
SEG_DEV = 5
EPS = 1e-05
THETA = 10000.0


def from_behind(block, axis, distance):
    devices = range(lax.axis_size(axis))
    route = [(i - distance, i) for i in devices if i - distance in devices]
    return lax.ppermute(block, axis, route)


def rms_norm(row_block, gain_vec):
    widened = row_block.astype(jnp.float32)
    inverse_rms = lax.rsqrt(jnp.mean(widened * widened, axis=-1, keepdims=True) + EPS)
    return (widened * inverse_rms * gain_vec.astype(jnp.float32)).astype(jnp.bfloat16)


def prompt_index(positions, lengths):
    prompt_ends = jnp.cumsum(lengths)
    prompt_starts = prompt_ends - lengths
    inside = (positions[:, None] >= prompt_starts[None, :]).astype(jnp.int32)
    segment = jnp.sum(inside, axis=1) - 1
    members = jnp.arange(lengths.shape[0], dtype=jnp.int32)[None, :] == segment[:, None]
    offset = positions - jnp.sum(jnp.where(members, prompt_starts[None, :], 0), axis=1)
    return (segment, offset, members)


def slot_lookup(adapter, adapter_slot):
    matches = jnp.arange(adapter_slot.shape[0], dtype=jnp.int32)[None, :] == adapter[:, None]
    return jnp.sum(jnp.where(matches, adapter_slot[None, :], 0), axis=1)


def rotate(vectors, offset):
    half_dim = vectors.shape[-1] // 2
    frequency = jnp.exp(
        jnp.arange(half_dim, dtype=jnp.float32) * (-2.0 * math.log(THETA) / vectors.shape[-1])
    )
    angles = offset.astype(jnp.float32)[:, None] * frequency[None, :]
    cosine = jnp.cos(angles)[:, None, :]
    sine_table = jnp.sin(angles)[:, None, :]
    first_half = vectors[..., :half_dim]
    second_half = vectors[..., half_dim:]
    return jnp.concatenate(
        [
            first_half * cosine - second_half * sine_table,
            second_half * cosine + first_half * sine_table,
        ],
        axis=-1,
    )


def adapter_terms(row_block, code_rows, a_in, pieces):
    table_count, rank_cols, in_width = a_in.shape
    projected = lax.dot_general(
        row_block,
        a_in.reshape(table_count * rank_cols, in_width),
        (((1,), (1,)), ((), ())),
        preferred_element_type=jnp.float32,
    )
    chosen = (jnp.arange(table_count, dtype=jnp.int32)[None, :] == code_rows[:, None]).astype(
        jnp.float32
    )
    low_rank = (projected.reshape(-1, table_count, rank_cols) * chosen[:, :, None]).astype(
        jnp.bfloat16
    )
    results = []
    for col_start, b_table in pieces:
        width_rank = b_table.shape[1]
        section = low_rank[:, :, col_start : col_start + width_rank].reshape(
            -1, table_count * width_rank
        )
        results.append(
            jnp.dot(
                section,
                b_table.reshape(table_count * width_rank, b_table.shape[2]),
                preferred_element_type=jnp.float32,
            ).astype(jnp.bfloat16)
        )
    return tuple(results)


def on_device(
    tokens,
    norm_gain,
    w_query,
    w_key,
    w_value,
    w_output,
    qkv_in,
    q_out,
    kv_out,
    o_in,
    o_out,
    lengths,
    prompt_adapter,
    adapter_slot,
):
    tok_rows = tokens.shape[0]
    tok_count = lax.axis_size("tok")
    own_count = lax.axis_size("own")
    per_owner = qkv_in.shape[0]
    device_here = lax.axis_index(("tok", "own"))
    positions = device_here * tok_rows + jnp.arange(tok_rows, dtype=jnp.int32)
    segment, offset, members = prompt_index(positions, lengths)
    prompt_count = lengths.shape[0]
    first_segment = segment[0]
    code_rows = segment - first_segment
    normed = rms_norm(tokens, norm_gain)
    tables = (qkv_in, q_out, kv_out, o_in, o_out)
    table_shapes = tuple((table.shape[1:] for table in tables))
    packed = jnp.concatenate([table.reshape(per_owner, -1) for table in tables], axis=1)
    all_slots = lax.all_gather(packed, "own", axis=0, tiled=True)
    own_here = lax.axis_index("own")
    group_blocks = jnp.arange(tok_count, dtype=jnp.int32) * own_count + own_here
    prompt_starts = jnp.cumsum(lengths) - lengths
    group_first = (
        jnp.sum(
            (group_blocks[:, None] * tok_rows >= prompt_starts[None, :]).astype(jnp.int32), axis=1
        )
        - 1
    )
    group_segments = jnp.minimum(
        group_first[:, None] + jnp.arange(SEG_DEV, dtype=jnp.int32)[None, :], prompt_count - 1
    )
    group_slots = jnp.take(adapter_slot, jnp.take(prompt_adapter, group_segments))
    outgoing = jnp.take(all_slots, group_slots.reshape(-1), axis=0).reshape(
        tok_count, SEG_DEV, packed.shape[1]
    )
    incoming = lax.all_to_all(outgoing, "tok", 0, 0, tiled=True)
    selected = []
    col = 0
    for table_shape in table_shapes:
        width = table_shape[0] * table_shape[1]
        piece = incoming[:, :, col : col + width].reshape(
            tok_count, SEG_DEV, table_shape[0], table_shape[1]
        )
        col += width
        selected.append(
            jnp.transpose(piece, (1, 2, 0, 3)).reshape(
                SEG_DEV, table_shape[0], tok_count * table_shape[1]
            )
        )
    input_maps, query_maps, keyvalue_maps, output_in_maps, output_out_maps = selected
    delta_q, delta_k, delta_v = adapter_terms(
        normed,
        code_rows,
        input_maps,
        ((0, query_maps), (RANK, keyvalue_maps[:, :RANK]), (2 * RANK, keyvalue_maps[:, RANK:])),
    )
    base_q = jnp.dot(normed, w_query, preferred_element_type=jnp.float32)
    base_k = jnp.dot(normed, w_key, preferred_element_type=jnp.float32)
    base_v = jnp.dot(normed, w_value, preferred_element_type=jnp.float32)
    query_lin = (base_q + delta_q.astype(jnp.float32)).reshape(tok_rows, HEADS, HEAD_WIDTH)
    queries = rotate(query_lin, offset).reshape(tok_rows, D).astype(jnp.bfloat16)
    key_lin = (base_k + delta_k.astype(jnp.float32)).reshape(tok_rows, KV_HEADS, HEAD_WIDTH)
    key_rows = rotate(key_lin, offset).reshape(tok_rows, KVW).astype(jnp.bfloat16)
    value_rows = (base_v + delta_v.astype(jnp.float32)).astype(jnp.bfloat16)
    key_value = jnp.concatenate([key_rows, value_rows], axis=1)
    key_store = jnp.zeros(((REACH + 1) * tok_rows, 2 * KVW), jnp.bfloat16)
    key_store = lax.dynamic_update_slice_in_dim(key_store, key_value, REACH * tok_rows, 0)
    window = key_store
    moving = key_value
    for turn_index in range(REACH):
        moving = from_behind(moving, ("tok", "own"), 1)
        window = lax.dynamic_update_slice_in_dim(
            window, moving, (REACH - 1 - turn_index) * tok_rows, 0
        )
    key_positions = (
        device_here * tok_rows
        - REACH * tok_rows
        + jnp.arange((REACH + 1) * tok_rows, dtype=jnp.int32)
    )
    key_segment = prompt_index(key_positions, lengths)[0]
    allowed = (segment[:, None] == key_segment[None, :]) & (
        key_positions[None, :] <= positions[:, None]
    )
    groups = HEADS // KV_HEADS
    key_count = window.shape[0]
    query_head_rows = queries.reshape(tok_rows, KV_HEADS, groups, HEAD_WIDTH)
    key_head_rows = window[:, :KVW].reshape(key_count, KV_HEADS, HEAD_WIDTH)
    value_head_rows = window[:, KVW:].reshape(key_count, KV_HEADS, HEAD_WIDTH)
    score_matrix = jnp.einsum(
        "qkzr,ckr->kzqc", query_head_rows, key_head_rows, preferred_element_type=jnp.float32
    ) * HEAD_WIDTH ** (-0.5)
    score_matrix = jnp.where(allowed[None, None], score_matrix, -1e30)
    top_score = jnp.max(score_matrix, axis=-1, keepdims=True)
    exp_scores = jnp.exp(score_matrix - top_score)
    row_total = jnp.sum(exp_scores, axis=-1)
    rounded_values = exp_scores.astype(jnp.bfloat16)
    summed_rows = jnp.einsum(
        "iyxv,vip->xiyp", rounded_values, value_head_rows, preferred_element_type=jnp.float32
    )
    attn_rows = (
        (summed_rows / jnp.transpose(row_total, (2, 0, 1))[..., None])
        .reshape(tok_rows, D)
        .astype(jnp.bfloat16)
    )
    delta_o = adapter_terms(attn_rows, code_rows, output_in_maps, ((0, output_out_maps),))[0]
    projected_out = jnp.dot(
        attn_rows, w_output, preferred_element_type=jnp.float32
    ) + delta_o.astype(jnp.float32)
    mixed_rows = (tokens.astype(jnp.float32) + projected_out).astype(jnp.bfloat16)
    return (mixed_rows, key_value)


def solution(mesh):
    return jax.shard_map(
        on_device,
        mesh=mesh,
        in_specs=(
            P(("tok", "own"), None),
            P(),
            P(),
            P(),
            P(),
            P(),
            P("own", None, "tok"),
            P("own", None, "tok"),
            P("own", None, "tok"),
            P("own", None, "tok"),
            P("own", None, "tok"),
            P(),
            P(),
            P(),
        ),
        out_specs=(P(("tok", "own"), None), P(("tok", "own"), None)),
        check_vma=False,
    )
```

profile of v0, /device:TPU:24, one launch (start us, length us, event | category | flops | bytes accessed | tf_op | source)
XLA Modules:
  0.0 273.8 jit_solution(17576496565474559692)
XLA Ops:
  0.7 1.0 reshape.328
  5.4 1.2 gather_fusion.1
  7.0 1.2 gather_fusion.2
  9.0 15.0 %all_gather.3 = bf16[64,7680]{1,0:T(8,128)(2,1)} all-gather(bf16[8,7680]{1,0:T(8,128)(2,1)S(1)} %constant_dynamic-update-slice_fusion), channel_id=1, replica_groups=mesh['tok'=16,'own'=8] {'own'}, dimensions={0}, use_global_device_ids=true | all-gather | bytes 1105920 | tf_op jit(solution)/shard_map/all_gather | solution.py:125
  24.0 4.8 %gather_fusion = bf16[80,7680]{1,0:T(8,128)(2,1)} fusion(bf16[64,7680]{1,0:T(8,128)(2,1)} %all_gather.3, s32[1024]{0:T(1024)S(1)} %pad_clamp_fusion), kind=kCustom, calls=%fused_computation.2 | custom fusion | bytes 2457920 | tf_op jit(solution)/shard_map/jit(_take)/gather | solution.py:139
  28.8 2.6 gather.10
  31.5 3.1 %broadcast_select_fusion = bf16[16,5,7680]{2,1,0:T(8,128)(2,1)} fusion(bf16[16,5,7680]{2,1,0:T(8,128)(2,1)} %gather.10, pred[16,5]{1,0:T(8,128)(4,1)S(1)} %get-tuple-element.3), kind=kLoop, calls=%fused_computation.18 | loop fusion | flops 614400 | bytes 2457680 | tf_op jit(solution)/shard_map/jit(_take)/select_n | solution.py:139
  34.6 8.3 %all-to-all-start = ((bf16[16,5,7680]{2,1,0:T(8,128)(2,1)}), bf16[16,5,7680]{2,1,0:T(8,128)(2,1)}, u32[]{:S(2)}, u32[]{:S(2)}) async-start(bf16[16,5,7680]{2,1,0:T(8,128)(2,1)} %broadcast_select_fusion), calls=%async_computation | async-start | bytes 3932160 | tf_op jit(solution)/shard_map/all_to_all | solution.py:142
  44.9 25.3 %all-to-all-done = bf16[16,5,7680]{2,1,0:T(8,128)(2,1)} async-done(((bf16[16,5,7680]{2,1,0:T(8,128)(2,1)}), bf16[16,5,7680]{2,1,0:T(8,128)(2,1)}, u32[]{:S(2)}, u32[]{:S(2)}) %all-to-all-start) | async-done | bytes 1228832 | tf_op jit(solution)/shard_map/all_to_all | solution.py:142
  71.2 1.9 reshape.334
  73.0 2.2 copy.47
  75.2 2.3 reshape.335
  77.6 1.2 slice.74
  78.9 2.7 reshape.333
  81.5 2.4 copy.45
  84.0 2.2 dot_general.41
  86.6 1.1 fusion.17
  87.7 1.0 fusion.14
  88.8 1.6 convolution_add_fusion.3
  91.4 1.6 fusion.15
  93.0 1.9 collective-permute-start
  95.0 9.3 %collective-permute-done = bf16[128,768]{1,0:T(8,128)(2,1)S(1)} collective-permute-done((bf16[128,768]{1,0:T(8,128)(2,1)S(1)}, bf16[128,768]{1,0:T(8,128)(2,1)S(1)}, u32[]{:S(2)}, u32[]{:S(2)}) %collective-permute-start) | collective-permute-done | bytes 196640 | tf_op jit(solution)/shard_map/ppermute | solution.py:22
  104.2 2.1 collective-permute-start.1
  106.4 1.0 compare_and_fusion
  107.4 8.1 %collective-permute-done.1 = bf16[128,768]{1,0:T(8,128)(2,1)} collective-permute-done((bf16[128,768]{1,0:T(8,128)(2,1)S(1)}, bf16[128,768]{1,0:T(8,128)(2,1)}, u32[]{:S(2)}, u32[]{:S(2)}) %collective-permute-start.1) | collective-permute-done | bytes 196640 | tf_op jit(solution)/shard_map/ppermute | solution.py:22
  115.5 1.9 collective-permute-start.2
  117.5 2.0 fusion.43
  119.5 1.3 slice.84
  121.5 1.5 reshape.344
  123.8 2.0 reshape_reshape.9
  125.8 1.7 copy.56
  127.4 1.5 reshape.342
  129.8 2.0 dot_general.51
  131.7 1.7 copy.52
  133.4 1.5 reshape.340
  135.7 1.3 reshape_reshape.8
  137.0 1.9 collective-permute-start.3
  138.9 1.0 fusion.9
  139.9 8.5 %collective-permute-done.3 = bf16[128,768]{1,0:T(8,128)(2,1)S(1)} collective-permute-done((bf16[128,768]{1,0:T(8,128)(2,1)}, bf16[128,768]{1,0:T(8,128)(2,1)S(1)}, u32[]{:S(2)}, u32[]{:S(2)}) %collective-permute-start.3) | collective-permute-done | bytes 196640 | tf_op jit(solution)/shard_map/ppermute | solution.py:22
  148.4 1.9 collective-permute-start.4
  150.3 2.2 convolution_add_fusion.1
  152.5 2.1 copy.54
  154.9 4.8 %collective-permute-done.4 = bf16[128,768]{1,0:T(8,128)(2,1)} collective-permute-done((bf16[128,768]{1,0:T(8,128)(2,1)S(1)}, bf16[128,768]{1,0:T(8,128)(2,1)}, u32[]{:S(2)}, u32[]{:S(2)}) %collective-permute-start.4) | collective-permute-done | bytes 196640 | tf_op jit(solution)/shard_map/ppermute | solution.py:22
  159.7 1.9 collective-permute-start.5
  161.8 9.4 %collective-permute-done.5 = bf16[128,768]{1,0:T(8,128)(2,1)S(1)} collective-permute-done((bf16[128,768]{1,0:T(8,128)(2,1)}, bf16[128,768]{1,0:T(8,128)(2,1)S(1)}, u32[]{:S(2)}, u32[]{:S(2)}) %collective-permute-start.5) | collective-permute-done | bytes 196640 | tf_op jit(solution)/shard_map/ppermute | solution.py:22
  171.1 1.9 collective-permute-start.6
  173.1 9.2 %collective-permute-done.6 = bf16[128,768]{1,0:T(8,128)(2,1)S(1)} collective-permute-done((bf16[128,768]{1,0:T(8,128)(2,1)S(1)}, bf16[128,768]{1,0:T(8,128)(2,1)S(1)}, u32[]{:S(2)}, u32[]{:S(2)}) %collective-permute-start.6) | collective-permute-done | bytes 196640 | tf_op jit(solution)/shard_map/ppermute | solution.py:22
  182.3 1.9 collective-permute-start.7
  186.1 7.4 %collective-permute-done.7 = bf16[128,768]{1,0:T(8,128)(2,1)S(1)} collective-permute-done((bf16[128,768]{1,0:T(8,128)(2,1)S(1)}, bf16[128,768]{1,0:T(8,128)(2,1)S(1)}, u32[]{:S(2)}, u32[]{:S(2)}) %collective-permute-start.7) | collective-permute-done | bytes 196640 | tf_op jit(solution)/shard_map/ppermute | solution.py:22
  193.5 1.9 collective-permute-start.8
  196.4 8.3 %collective-permute-done.8 = bf16[128,768]{1,0:T(8,128)(2,1)S(1)} collective-permute-done((bf16[128,768]{1,0:T(8,128)(2,1)S(1)}, bf16[128,768]{1,0:T(8,128)(2,1)S(1)}, u32[]{:S(2)}, u32[]{:S(2)}) %collective-permute-start.8) | collective-permute-done | bytes 196640 | tf_op jit(solution)/shard_map/ppermute | solution.py:22
  204.7 1.9 collective-permute-start.9
  206.7 9.2 %collective-permute-done.9 = bf16[128,768]{1,0:T(8,128)(2,1)S(1)} collective-permute-done((bf16[128,768]{1,0:T(8,128)(2,1)S(1)}, bf16[128,768]{1,0:T(8,128)(2,1)S(1)}, u32[]{:S(2)}, u32[]{:S(2)}) %collective-permute-start.9) | collective-permute-done | bytes 196640 | tf_op jit(solution)/shard_map/ppermute | solution.py:22
  215.9 1.9 collective-permute-start.10
  217.9 9.2 %collective-permute-done.10 = bf16[128,768]{1,0:T(8,128)(2,1)S(1)} collective-permute-done((bf16[128,768]{1,0:T(8,128)(2,1)S(1)}, bf16[128,768]{1,0:T(8,128)(2,1)S(1)}, u32[]{:S(2)}, u32[]{:S(2)}) %collective-permute-start.10) | collective-permute-done | bytes 196640 | tf_op jit(solution)/shard_map/ppermute | solution.py:22
  227.1 1.9 collective-permute-start.11
  229.1 9.2 %collective-permute-done.11 = bf16[128,768]{1,0:T(8,128)(2,1)S(1)} collective-permute-done((bf16[128,768]{1,0:T(8,128)(2,1)S(1)}, bf16[128,768]{1,0:T(8,128)(2,1)S(1)}, u32[]{:S(2)}, u32[]{:S(2)}) %collective-permute-start.11) | collective-permute-done | bytes 196640 | tf_op jit(solution)/shard_map/ppermute | solution.py:22
  238.3 1.7 fusion.42
  240.1 2.5 copy.51
  242.6 2.5 copy.50
  245.1 9.0 %fusion.2 = (f32[6,3,128]{2,1,0:T(4,128)S(1)}, f32[6,1664,128,3]{2,1,3,0:T(8,128)}) fusion(pred[128,1664]{0,1:T(8,128)(4,1)S(1)} %compare_and_fusion, bf16[1664,6,64,1]{0,2,3,1:T(8,128)(2,1)} %bitcast.101, bf16[128,6,3,64]{0,3,2,1:T(8,128)(2,1)S(1)} %bitcast.105), kind=kOutput, calls=%fused_computation.7 | convolution fusion | flops 502232832 | bytes 17130496 | tf_op jit(solution)/shard_map/qkzr,ckr->kzqc/dot_general | solution.py:195
  254.0 8.6 %fusion = f32[6,3,128]{2,1,0:T(4,128)S(1)} fusion(f32[6,1664,128,3]{2,1,3,0:T(8,128)} %get-tuple-element.17, f32[6,3,128]{2,1,0:T(4,128)S(1)} %get-tuple-element.16, pred[128,1664]{0,1:T(8,128)(4,1)S(1)} %compare_and_fusion), kind=kLoop, calls=%fused_computation.5 | loop fusion | flops 15333120 | bytes 15566848 | tf_op jit(solution)/shard_map/reduce_sum | solution.py:201
  262.7 9.2 %fusion.23 = bf16[128,6,3,64]{0,3,2,1:T(8,128)(2,1)S(1)} fusion(bf16[1664,6,64,1]{0,2,3,1:T(8,128)(2,1)S(1)} %bitcast.109, f32[6,1664,128,3]{2,1,3,0:T(8,128)} %get-tuple-element.17, f32[6,3,128]{2,1,0:T(4,128)S(1)} %get-tuple-element.16, pred[128,1664]{0,1:T(8,128)(4,1)S(1)} %compare_and_fusion, f32[128,6,3]{0,2,1:T(4,128)S(1)} %bitcast.116), kind=kOutput, calls=%fused_computation.34 | convolution fusion | flops 506363904 | bytes 17139712 | tf_op jit(solution)/shard_map/iyxv,vip->xiyp/dot_general | solution.py:203
  272.4 1.3 fusion.7
  (141 shorter events, 16.0 us)
Async XLA Ops:
  0.6 149.7 %copy-start = (bf16[1152,1152]{1,0:T(8,128)(2,1)S(1)}, bf16[1152,1152]{1,0:T(8,128)(2,1)}, u32[]{:S(2)}) copy-start(bf16[1152,1152]{1,0:T(8,128)(2,1)} %param.18) | copy-start | bytes 7962628
  0.6 4.8 %copy-start.1 = (s32[64]{0:T(128)S(1)}, s32[64]{0:T(128)}, u32[]{:S(2)}) copy-start(s32[64]{0:T(128)} %param.28) | copy-start | bytes 772
  5.4 1.5 copy-start.2
  7.0 1.6 copy-start.19
  7.0 1.7 copy-start.23
  34.6 8.3 %copy-start.3 = (bf16[128,1152]{1,0:T(8,128)(2,1)S(1)}, bf16[128,1152]{1,0:T(8,128)(2,1)}, u32[]{:S(2)}) copy-start(bf16[128,1152]{1,0:T(8,128)(2,1)} %param.16) | copy-start | bytes 884740
  34.6 9.4 %copy-start.26 = (bf16[1152]{0:T(1024)(128)(2,1)S(1)}, bf16[1152]{0:T(1024)(128)(2,1)}, u32[]{:S(2)}) copy-start(bf16[1152]{0:T(1024)(128)(2,1)} %param.17) | copy-start | bytes 6916
  34.6 35.6 %all-to-all-start = ((bf16[16,5,7680]{2,1,0:T(8,128)(2,1)}), bf16[16,5,7680]{2,1,0:T(8,128)(2,1)}, u32[]{:S(2)}, u32[]{:S(2)}) async-start(bf16[16,5,7680]{2,1,0:T(8,128)(2,1)} %broadcast_select_fusion), calls=%async_computation | async-start | bytes 3932160 | tf_op jit(solution)/shard_map/all_to_all | solution.py:142
  42.9 27.3 %copy-start.29 = (s32[128]{0:T(128)}, s32[128]{0:T(128)S(1)}, u32[]{:S(2)}) copy-start(s32[128]{0:T(128)S(1)} %iota_add_fusion.1) | copy-start | bytes 1540
  43.1 1.0 copy-start.20
  43.2 27.0 %copy-start.31 = (s32[128]{0:T(128)}, s32[128]{0:T(128)S(1)}, u32[]{:S(2)}) copy-start(s32[128]{0:T(128)S(1)} %broadcast_add_fusion.1) | copy-start | bytes 1540
  44.0 42.1 %copy-start.18 = (f32[1152]{0:T(1024)}, f32[1152]{0:T(1024)S(1)}, u32[]{:S(2)}) copy-start(f32[1152]{0:T(1024)S(1)} %convert_element_type.91) | copy-start | bytes 13828
  44.1 42.1 %copy-start.25 = (f32[128]{0:T(128)}, f32[128]{0:T(128)S(1)}, u32[]{:S(2)}) copy-start(f32[128]{0:T(128)S(1)} %add_rsqrt_fusion) | copy-start | bytes 1540
  44.1 42.0 %copy-start.27 = (f32[128,5]{0,1:T(8,128)}, f32[128,5]{0,1:T(8,128)S(1)}, u32[]{:S(2)}) copy-start(f32[128,5]{0,1:T(8,128)S(1)} %fusion.34) | copy-start | bytes 7684
  44.9 45.6 %copy-start.15 = (f32[128,32]{0,1:T(8,128)}, f32[128,32]{0,1:T(8,128)S(1)}, u32[]{:S(2)}) copy-start(f32[128,32]{0,1:T(8,128)S(1)} %get-tuple-element.14) | copy-start | bytes 49156
  86.6 2.1 copy-start.22
  90.5 4.5 %copy-start.24 = (s32[1664]{0:T(1024)S(1)}, s32[1664]{0:T(1024)}, u32[]{:S(2)}) copy-start(s32[1664]{0:T(1024)} %convert_reduce_fusion) | copy-start | bytes 19972
  90.5 15.9 %copy-start.21 = (s32[1664]{0:T(1024)S(1)}, s32[1664]{0:T(1024)}, u32[]{:S(2)}) copy-start(s32[1664]{0:T(1024)} %copy-done.20) | copy-start | bytes 19972
  90.5 15.9 %copy-start.30 = (s32[128]{0:T(128)S(1)}, s32[128]{0:T(128)}, u32[]{:S(2)}) copy-start(s32[128]{0:T(128)} %copy-done.29) | copy-start | bytes 1540
  90.5 15.9 %copy-start.32 = (s32[128]{0:T(128)S(1)}, s32[128]{0:T(128)}, u32[]{:S(2)}) copy-start(s32[128]{0:T(128)} %copy-done.31) | copy-start | bytes 1540
  93.0 22.5 %copy-start.7 = (bf16[128,768]{1,0:T(8,128)(2,1)}, bf16[128,768]{1,0:T(8,128)(2,1)S(1)}, u32[]{:S(2)}) copy-start(bf16[128,768]{1,0:T(8,128)(2,1)S(1)} %pad_maximum_fusion.1) | copy-start | bytes 589828
  93.0 11.2 %collective-permute-start = (bf16[128,768]{1,0:T(8,128)(2,1)S(1)}, bf16[128,768]{1,0:T(8,128)(2,1)S(1)}, u32[]{:S(2)}, u32[]{:S(2)}) collective-permute-start(bf16[128,768]{1,0:T(8,128)(2,1)S(1)} %pad_maximum_fusion.1), channel_id=1, source_target_pairs={{0,1},{1,2},{2,3},{3,4},{4,5},{5,6},{6,7},{7,8},{8,9},{9,10},{10,1... | collective-permute-start | bytes 589832 | tf_op jit(solution)/shard_map/ppermute | solution.py:22
  104.2 11.3 %copy-start.10 = (bf16[128,768]{1,0:T(8,128)(2,1)}, bf16[128,768]{1,0:T(8,128)(2,1)S(1)}, u32[]{:S(2)}) copy-start(bf16[128,768]{1,0:T(8,128)(2,1)S(1)} %collective-permute-done) | copy-start | bytes 589828
  104.2 11.3 %collective-permute-start.1 = (bf16[128,768]{1,0:T(8,128)(2,1)S(1)}, bf16[128,768]{1,0:T(8,128)(2,1)}, u32[]{:S(2)}, u32[]{:S(2)}) collective-permute-start(bf16[128,768]{1,0:T(8,128)(2,1)S(1)} %collective-permute-done), channel_id=1, source_target_pairs={{0,1},{1,2},{2,3},{3,4},{4,5},{5,6},{6,7},{7,8},{8,9},{9,10},{10,1... | collective-permute-start | bytes 589832 | tf_op jit(solution)/shard_map/ppermute | solution.py:22
  115.5 21.4 %collective-permute-start.2 = (bf16[128,768]{1,0:T(8,128)(2,1)}, bf16[128,768]{1,0:T(8,128)(2,1)}, u32[]{:S(2)}, u32[]{:S(2)}) collective-permute-start(bf16[128,768]{1,0:T(8,128)(2,1)} %collective-permute-done.1), channel_id=1, source_target_pairs={{0,1},{1,2},{2,3},{3,4},{4,5},{5,6},{6,7},{7,8},{8,9},{9,10},{10,1... | collective-permute-start | bytes 589832 | tf_op jit(solution)/shard_map/ppermute | solution.py:22
  137.0 11.4 %collective-permute-start.3 = (bf16[128,768]{1,0:T(8,128)(2,1)}, bf16[128,768]{1,0:T(8,128)(2,1)S(1)}, u32[]{:S(2)}, u32[]{:S(2)}) collective-permute-start(bf16[128,768]{1,0:T(8,128)(2,1)} %collective-permute-done.2), channel_id=1, source_target_pairs={{0,1},{1,2},{2,3},{3,4},{4,5},{5,6},{6,7},{7,8},{8,9},{9,10},{10,1... | collective-permute-start | bytes 589832 | tf_op jit(solution)/shard_map/ppermute | solution.py:22
  139.9 14.8 %copy-start.8 = (bf16[128,768]{1,0:T(8,128)(2,1)S(1)}, bf16[128,768]{1,0:T(8,128)(2,1)}, u32[]{:S(2)}) copy-start(bf16[128,768]{1,0:T(8,128)(2,1)} %copy-done.7) | copy-start | bytes 589828
  148.4 6.2 %copy-start.12 = (bf16[128,768]{1,0:T(8,128)(2,1)}, bf16[128,768]{1,0:T(8,128)(2,1)S(1)}, u32[]{:S(2)}) copy-start(bf16[128,768]{1,0:T(8,128)(2,1)S(1)} %collective-permute-done.3) | copy-start | bytes 589828
  148.4 11.3 %collective-permute-start.4 = (bf16[128,768]{1,0:T(8,128)(2,1)S(1)}, bf16[128,768]{1,0:T(8,128)(2,1)}, u32[]{:S(2)}, u32[]{:S(2)}) collective-permute-start(bf16[128,768]{1,0:T(8,128)(2,1)S(1)} %collective-permute-done.3), channel_id=1, source_target_pairs={{0,1},{1,2},{2,3},{3,4},{4,5},{5,6},{6,7},{7,8},{8,9},{9,10},{10,1... | collective-permute-start | bytes 589832 | tf_op jit(solution)/shard_map/ppermute | solution.py:22
  154.7 7.0 %copy-start.5 = (f32[128,1152]{0,1:T(8,128)S(1)}, f32[128,1152]{0,1:T(8,128)}, u32[]{:S(2)}) copy-start(f32[128,1152]{0,1:T(8,128)} %copy.54) | copy-start | bytes 1769476
  154.7 7.0 %copy-start.16 = (f32[128,32]{0,1:T(8,128)S(1)}, f32[128,32]{0,1:T(8,128)}, u32[]{:S(2)}) copy-start(f32[128,32]{0,1:T(8,128)} %copy-done.15) | copy-start | bytes 49156
  154.7 7.0 %copy-start.17 = (f32[128,32]{0,1:T(8,128)S(1)}, f32[128,32]{0,1:T(8,128)}, u32[]{:S(2)}) copy-start(f32[128,32]{0,1:T(8,128)} %get-tuple-element.15) | copy-start | bytes 49156
  154.7 18.4 %copy-start.11 = (bf16[128,768]{1,0:T(8,128)(2,1)S(1)}, bf16[128,768]{1,0:T(8,128)(2,1)}, u32[]{:S(2)}) copy-start(bf16[128,768]{1,0:T(8,128)(2,1)} %copy-done.10) | copy-start | bytes 589828
  154.9 40.6 %copy-start.13 = (bf16[128,768]{1,0:T(8,128)(2,1)S(1)}, bf16[128,768]{1,0:T(8,128)(2,1)}, u32[]{:S(2)}) copy-start(bf16[128,768]{1,0:T(8,128)(2,1)} %copy-done.12) | copy-start | bytes 589828
  159.7 11.4 %collective-permute-start.5 = (bf16[128,768]{1,0:T(8,128)(2,1)}, bf16[128,768]{1,0:T(8,128)(2,1)S(1)}, u32[]{:S(2)}, u32[]{:S(2)}) collective-permute-start(bf16[128,768]{1,0:T(8,128)(2,1)} %collective-permute-done.4), channel_id=1, source_target_pairs={{0,1},{1,2},{2,3},{3,4},{4,5},{5,6},{6,7},{7,8},{8,9},{9,10},{10,1... | collective-permute-start | bytes 589832 | tf_op jit(solution)/shard_map/ppermute | solution.py:22
  171.1 11.2 %collective-permute-start.6 = (bf16[128,768]{1,0:T(8,128)(2,1)S(1)}, bf16[128,768]{1,0:T(8,128)(2,1)S(1)}, u32[]{:S(2)}, u32[]{:S(2)}) collective-permute-start(bf16[128,768]{1,0:T(8,128)(2,1)S(1)} %collective-permute-done.5), channel_id=1, source_target_pairs={{0,1},{1,2},{2,3},{3,4},{4,5},{5,6},{6,7},{7,8},{8,9},{9,10},{10,1... | collective-permute-start | bytes 589832 | tf_op jit(solution)/shard_map/ppermute | solution.py:22
  182.3 11.2 %collective-permute-start.7 = (bf16[128,768]{1,0:T(8,128)(2,1)S(1)}, bf16[128,768]{1,0:T(8,128)(2,1)S(1)}, u32[]{:S(2)}, u32[]{:S(2)}) collective-permute-start(bf16[128,768]{1,0:T(8,128)(2,1)S(1)} %collective-permute-done.6), channel_id=1, source_target_pairs={{0,1},{1,2},{2,3},{3,4},{4,5},{5,6},{6,7},{7,8},{8,9},{9,10},{10,1... | collective-permute-start | bytes 589832 | tf_op jit(solution)/shard_map/ppermute | solution.py:22
  193.5 11.2 %collective-permute-start.8 = (bf16[128,768]{1,0:T(8,128)(2,1)S(1)}, bf16[128,768]{1,0:T(8,128)(2,1)S(1)}, u32[]{:S(2)}, u32[]{:S(2)}) collective-permute-start(bf16[128,768]{1,0:T(8,128)(2,1)S(1)} %collective-permute-done.7), channel_id=1, source_target_pairs={{0,1},{1,2},{2,3},{3,4},{4,5},{5,6},{6,7},{7,8},{8,9},{9,10},{10,1... | collective-permute-start | bytes 589832 | tf_op jit(solution)/shard_map/ppermute | solution.py:22
  204.7 11.2 %collective-permute-start.9 = (bf16[128,768]{1,0:T(8,128)(2,1)S(1)}, bf16[128,768]{1,0:T(8,128)(2,1)S(1)}, u32[]{:S(2)}, u32[]{:S(2)}) collective-permute-start(bf16[128,768]{1,0:T(8,128)(2,1)S(1)} %collective-permute-done.8), channel_id=1, source_target_pairs={{0,1},{1,2},{2,3},{3,4},{4,5},{5,6},{6,7},{7,8},{8,9},{9,10},{10,1... | collective-permute-start | bytes 589832 | tf_op jit(solution)/shard_map/ppermute | solution.py:22
  215.9 11.2 %collective-permute-start.10 = (bf16[128,768]{1,0:T(8,128)(2,1)S(1)}, bf16[128,768]{1,0:T(8,128)(2,1)S(1)}, u32[]{:S(2)}, u32[]{:S(2)}) collective-permute-start(bf16[128,768]{1,0:T(8,128)(2,1)S(1)} %collective-permute-done.9), channel_id=1, source_target_pairs={{0,1},{1,2},{2,3},{3,4},{4,5},{5,6},{6,7},{7,8},{8,9},{9,10},{10,1... | collective-permute-start | bytes 589832 | tf_op jit(solution)/shard_map/ppermute | solution.py:22
  227.1 11.2 %collective-permute-start.11 = (bf16[128,768]{1,0:T(8,128)(2,1)S(1)}, bf16[128,768]{1,0:T(8,128)(2,1)S(1)}, u32[]{:S(2)}, u32[]{:S(2)}) collective-permute-start(bf16[128,768]{1,0:T(8,128)(2,1)S(1)} %collective-permute-done.10), channel_id=1, source_target_pairs={{0,1},{1,2},{2,3},{3,4},{4,5},{5,6},{6,7},{7,8},{8,9},{9,10},{10,1... | collective-permute-start | bytes 589832 | tf_op jit(solution)/shard_map/ppermute | solution.py:22
  254.0 8.6 %copy-start.6 = (bf16[1664,384]{0,1:T(8,128)(2,1)S(1)}, bf16[1664,384]{0,1:T(8,128)(2,1)}, u32[]{:S(2)}) copy-start(bf16[1664,384]{0,1:T(8,128)(2,1)} %copy.50) | copy-start | bytes 3833860
  262.7 9.3 %copy-start.14 = (bf16[5,16,1152]{2,1,0:T(8,128)(2,1)S(1)}, bf16[5,16,1152]{2,1,0:T(8,128)(2,1)}, u32[]{:S(2)}) copy-start(bf16[5,16,1152]{2,1,0:T(8,128)(2,1)} %dot_general.51) | copy-start | bytes 552964
  262.7 9.3 %copy-start.28 = (f32[128,5]{0,1:T(8,128)S(1)}, f32[128,5]{0,1:T(8,128)}, u32[]{:S(2)}) copy-start(f32[128,5]{0,1:T(8,128)} %copy-done.27) | copy-start | bytes 7684
  262.7 9.5 %copy-start.9 = (bf16[80,1152]{1,0:T(8,128)(2,1)S(1)}, bf16[80,1152]{1,0:T(8,128)(2,1)}, u32[]{:S(2)}) copy-start(bf16[80,1152]{1,0:T(8,128)(2,1)} %reshape_reshape.9) | copy-start | bytes 552964
  262.7 9.7 %copy-start.4 = (bf16[1152,1152]{1,0:T(8,128)(2,1)S(1)}, bf16[1152,1152]{1,0:T(8,128)(2,1)}, u32[]{:S(2)}) copy-start(bf16[1152,1152]{1,0:T(8,128)(2,1)} %param.21) | copy-start | bytes 7962628
where the time goes:
time: 276 us; the launch traced here: 274 us
  waiting for transfers between devices  118 us (43%)
  local copies, waits for them, and re-layouts  62.1 us (22%)
  starting transfers between devices  31.4 us (11%)
  matrix products  28.8 us (10%)
  other arithmetic  16.9 us (6%)
  blocking collectives  15 us (5%)
    ppermute x12, waiting for transfers between devices, from_behind(): return lax.ppermute(block, axis, route)  92.7 us
    all_to_all x1, waiting for transfers between devices, on_device(): incoming = lax.all_to_all(outgoing, 'tok', 0, 0, tiled=True)  25.3 us
    ppermute x12, starting transfers between devices, from_behind(): return lax.ppermute(block, axis, route)  23.1 us
    all_gather x1, blocking collectives, on_device(): all_slots = lax.all_gather(packed, 'own', axis=0, tiled=True)  15 us
    dot_general x1, matrix products, on_device(): jnp.einsum('iyxv,vip->xiyp', rounded_values, value_head_rows, preferred_e...  9.21 us
    reshape x5, local copies, waits for them, and re-layouts, on_device(): incoming[:, :, col:col + width]  9 us
    dot_general x1, matrix products, on_device(): jnp.einsum('qkzr,ckr->kzqc', query_head_rows, key_head_rows, preferred_el...  8.99 us
    reduce_sum x1, other arithmetic, on_device(): row_total = jnp.sum(exp_scores, axis=-1)  8.61 us
  transfers between devices with their start and end apart: 13, of which 12 were waited for; matrix products, arithmetic and copies ran while one was open for 11% of the time, Pallas kernels for 0%

commit v1 on v0

--- a/solution.py
+++ b/solution.py
@@ -122,7 +122,24 @@
     tables = (qkv_in, q_out, kv_out, o_in, o_out)
     table_shapes = tuple((table.shape[1:] for table in tables))
     packed = jnp.concatenate([table.reshape(per_owner, -1) for table in tables], axis=1)
-    all_slots = lax.all_gather(packed, "own", axis=0, tiled=True)
+    devices_2, position, span = (lax.axis_size("own"), lax.axis_index("own"), packed.shape[0])
+    right = [(i_2, (i_2 + 1) % devices_2) for i_2 in range(devices_2)]
+    left = [(i_2, (i_2 - 1) % devices_2) for i_2 in range(devices_2)]
+    whole = jnp.zeros((*packed.shape[:0], devices_2 * span, *packed.shape[0 + 1 :]), packed.dtype)
+    whole = lax.dynamic_update_slice_in_dim(whole, packed, position * span, axis=0)
+    from_left = from_right = packed
+    middle = devices_2 // 2
+    for hop in range(1, middle + 1):
+        from_left = lax.ppermute(from_left, "own", right)
+        whole = lax.dynamic_update_slice_in_dim(
+            whole, from_left, (position - hop) % devices_2 * span, axis=0
+        )
+        if hop < devices_2 - middle:
+            from_right = lax.ppermute(from_right, "own", left)
+            whole = lax.dynamic_update_slice_in_dim(
+                whole, from_right, (position + hop) % devices_2 * span, axis=0
+            )
+    all_slots = whole
     own_here = lax.axis_index("own")
     group_blocks = jnp.arange(tok_count, dtype=jnp.int32) * own_count + own_here
     prompt_starts = jnp.cumsum(lengths) - lengths

time: 276 us -> 286 us (1.036)
  local copies, waits for them, and re-layouts: 62.1 us -> 80.5 us
  blocking collectives: 15 us -> 0 us
  starting transfers between devices: 31.4 us -> 39.8 us
  waiting for transfers between devices: 118 us -> 115 us
    all_gather x1 -> x0, blocking collectives: 15 us -> none  [on_device(): all_slots = lax.all_gather(packed, 'own', axis=0, tiled=True)]
    ppermute x0 -> x7, waiting for transfers between devices: none -> 9.54 us  [the longest x4 8.4 us: on_device(): from_left = lax.ppermute(from_left, 'own', right)]
    dynamic_update_slice x12, local copies, waits for them, and re-layouts: 2.96 us -> 12 us  [on_device(): lax.dynamic_update_slice_in_dim(window, moving, (REACH - 1 - turn_index)...]
    ppermute x0 -> x7, starting transfers between devices: none -> 8.23 us  [the longest x3 8.22 us: on_device(): from_right = lax.ppermute(from_right, 'own', left)]
    ppermute x12, waiting for transfers between devices: 92.7 us -> 84.5 us  [from_behind(): return lax.ppermute(block, axis, route)]
    dynamic_update_slice x0 -> x8, local copies, waits for them, and re-layouts: none -> 5.25 us  [the longest x4 2.62 us: on_device(): lax.dynamic_update_slice_in_dim(whole, from_left, (position - hop) % devi...]
    all_to_all x1, waiting for transfers between devices: 25.3 us -> 21.2 us  [on_device(): incoming = lax.all_to_all(outgoing, 'tok', 0, 0, tiled=True)]
  transfers between devices with their start and end apart: 13 -> 20, of which waited for: 12 -> 15; matrix products, arithmetic and copies ran while one was open for 11% -> 19% of each run, Pallas kernels for 0% -> 0%
where the time goes in v1:
time: 286 us; the launch traced here: 284 us
  waiting for transfers between devices  115 us (40%)
  local copies, waits for them, and re-layouts  80.5 us (28%)
  starting transfers between devices  39.8 us (14%)
  matrix products  28.1 us (10%)
  other arithmetic  18.9 us (7%)
    ppermute x12, waiting for transfers between devices, from_behind(): return lax.ppermute(block, axis, route)  84.5 us
    ppermute x12, starting transfers between devices, from_behind(): return lax.ppermute(block, axis, route)  23.2 us
    all_to_all x1, waiting for transfers between devices, on_device(): incoming = lax.all_to_all(outgoing, 'tok', 0, 0, tiled=True)  21.2 us
    dynamic_update_slice x12, local copies, waits for them, and re-layouts, on_device(): lax.dynamic_update_slice_in_dim(window, moving, (REACH - 1 - turn_index)...  12 us
    dot_general x1, matrix products, on_device(): jnp.einsum('iyxv,vip->xiyp', rounded_values, value_head_rows, preferred_e...  9.21 us
    dot_general x1, matrix products, on_device(): jnp.einsum('qkzr,ckr->kzqc', query_head_rows, key_head_rows, preferred_el...  8.99 us
    reduce_sum x1, other arithmetic, on_device(): row_total = jnp.sum(exp_scores, axis=-1)  8.61 us
    ppermute x4, waiting for transfers between devices, on_device(): from_left = lax.ppermute(from_left, 'own', right)  8.4 us
  transfers between devices with their start and end apart: 20, of which 15 were waited for; matrix products, arithmetic and copies ran while one was open for 19% of the time, Pallas kernels for 0%

profile of v1, /device:TPU:24, one launch (start us, length us, event | category | flops | bytes accessed | tf_op | source)
XLA Modules:
  0.0 283.9 jit_solution(1797261672248460899)
XLA Ops:
  5.6 2.2 collective-permute-start.1
  16.6 2.9 %collective-permute-start.3 = (bf16[8,7680]{1,0:T(8,128)(2,1)S(1)}, bf16[8,7680]{1,0:T(8,128)(2,1)S(1)}, u32[]{:S(2)}, u32[]{:S(2)}) collective-permute-start(bf16[8,7680]{1,0:T(8,128)(2,1)S(1)} %collective-permute-done.1), channel_id=1, source_target_pairs={{0,7},{1,0},{2,1},{3,2},{4,3},{5,4},{6,5},{7,6},{8,15},{9,8},{10,9... | collective-permute-start | bytes 368648 | tf_op jit(solution)/shard_map/ppermute | solution.py:138
  22.0 3.1 %collective-permute-start.5 = (bf16[8,7680]{1,0:T(8,128)(2,1)S(1)}, bf16[8,7680]{1,0:T(8,128)(2,1)S(1)}, u32[]{:S(2)}, u32[]{:S(2)}) collective-permute-start(bf16[8,7680]{1,0:T(8,128)(2,1)S(1)} %collective-permute-done.3), channel_id=1, source_target_pairs={{0,7},{1,0},{2,1},{3,2},{4,3},{5,4},{6,5},{7,6},{8,15},{9,8},{10,9... | collective-permute-start | bytes 368648 | tf_op jit(solution)/shard_map/ppermute | solution.py:138
  26.3 4.2 %collective-permute-done.4 = bf16[8,7680]{1,0:T(8,128)(2,1)S(1)} collective-permute-done((bf16[8,7680]{1,0:T(8,128)(2,1)S(1)}, bf16[8,7680]{1,0:T(8,128)(2,1)S(1)}, u32[]{:S(2)}, u32[]{:S(2)}) %collective-permute-start.4) | collective-permute-done | bytes 122912 | tf_op jit(solution)/shard_map/ppermute | solution.py:133
  31.9 4.2 %collective-permute-done.6 = bf16[8,7680]{1,0:T(8,128)(2,1)S(1)} collective-permute-done((bf16[8,7680]{1,0:T(8,128)(2,1)S(1)}, bf16[8,7680]{1,0:T(8,128)(2,1)S(1)}, u32[]{:S(2)}, u32[]{:S(2)}) %collective-permute-start.6) | collective-permute-done | bytes 122912 | tf_op jit(solution)/shard_map/ppermute | solution.py:133
  36.7 4.8 %gather_fusion = bf16[80,7680]{1,0:T(8,128)(2,1)} fusion(bf16[64,7680]{1,0:T(8,128)(2,1)} %constant_dynamic-update-slice_fusion.17, s32[1024]{0:T(1024)S(1)} %pad_clamp_fusion), kind=kCustom, calls=%fused_computation.2 | custom fusion | bytes 2457920 | tf_op jit(solution)/shard_map/jit(_take)/gather | solution.py:156
  41.5 2.6 gather.10
  44.2 3.1 %broadcast_select_fusion = bf16[16,5,7680]{2,1,0:T(8,128)(2,1)} fusion(bf16[16,5,7680]{2,1,0:T(8,128)(2,1)} %gather.10, pred[16,5]{1,0:T(8,128)(4,1)S(1)} %get-tuple-element.3), kind=kLoop, calls=%fused_computation.18 | loop fusion | flops 614400 | bytes 2457680 | tf_op jit(solution)/shard_map/jit(_take)/select_n | solution.py:156
  47.3 8.3 %all-to-all-start = ((bf16[16,5,7680]{2,1,0:T(8,128)(2,1)}), bf16[16,5,7680]{2,1,0:T(8,128)(2,1)}, u32[]{:S(2)}, u32[]{:S(2)}) async-start(bf16[16,5,7680]{2,1,0:T(8,128)(2,1)} %broadcast_select_fusion), calls=%async_computation | async-start | bytes 3932160 | tf_op jit(solution)/shard_map/all_to_all | solution.py:159
  56.5 21.2 %all-to-all-done = bf16[16,5,7680]{2,1,0:T(8,128)(2,1)} async-done(((bf16[16,5,7680]{2,1,0:T(8,128)(2,1)}), bf16[16,5,7680]{2,1,0:T(8,128)(2,1)}, u32[]{:S(2)}, u32[]{:S(2)}) %all-to-all-start) | async-done | bytes 1228832 | tf_op jit(solution)/shard_map/all_to_all | solution.py:159
  80.8 2.3 reshape.335
  83.1 1.2 slice.74
  84.5 2.7 reshape.333
  87.1 2.4 copy.45
  89.6 2.2 dot_general.41
  94.3 1.6 convolution_add_fusion.3
  97.0 1.6 fusion.15
  98.6 1.9 collective-permute-start.7
  100.6 9.3 %collective-permute-done.7 = bf16[128,768]{1,0:T(8,128)(2,1)S(1)} collective-permute-done((bf16[128,768]{1,0:T(8,128)(2,1)S(1)}, bf16[128,768]{1,0:T(8,128)(2,1)S(1)}, u32[]{:S(2)}, u32[]{:S(2)}) %collective-permute-start.7) | collective-permute-done | bytes 196640 | tf_op jit(solution)/shard_map/ppermute | solution.py:22
  109.8 1.9 collective-permute-start.8
  112.8 8.3 %collective-permute-done.8 = bf16[128,768]{1,0:T(8,128)(2,1)} collective-permute-done((bf16[128,768]{1,0:T(8,128)(2,1)S(1)}, bf16[128,768]{1,0:T(8,128)(2,1)}, u32[]{:S(2)}, u32[]{:S(2)}) %collective-permute-start.8) | collective-permute-done | bytes 196640 | tf_op jit(solution)/shard_map/ppermute | solution.py:22
  121.1 2.1 collective-permute-start.9
  123.2 2.0 fusion.43
  125.2 1.3 slice.84
  126.6 1.7 dynamic_update_slice.71
  128.9 1.5 reshape.344
  131.3 2.0 reshape_reshape.9
  133.3 1.7 copy.56
  134.9 1.5 reshape.342
  137.3 2.0 dot_general.51
  139.2 1.7 copy.52
  140.9 1.5 reshape.340
  143.2 1.3 reshape_reshape.8
  144.5 1.9 collective-permute-start.10
  147.5 8.5 %collective-permute-done.10 = bf16[128,768]{1,0:T(8,128)(2,1)S(1)} collective-permute-done((bf16[128,768]{1,0:T(8,128)(2,1)}, bf16[128,768]{1,0:T(8,128)(2,1)S(1)}, u32[]{:S(2)}, u32[]{:S(2)}) %collective-permute-start.10) | collective-permute-done | bytes 196640 | tf_op jit(solution)/shard_map/ppermute | solution.py:22
  156.0 1.9 collective-permute-start.11
  157.9 1.5 convolution_add_fusion.1
  159.4 2.1 copy.54
  161.5 5.8 %collective-permute-done.11 = bf16[128,768]{1,0:T(8,128)(2,1)} collective-permute-done((bf16[128,768]{1,0:T(8,128)(2,1)S(1)}, bf16[128,768]{1,0:T(8,128)(2,1)}, u32[]{:S(2)}, u32[]{:S(2)}) %collective-permute-start.11) | collective-permute-done | bytes 196640 | tf_op jit(solution)/shard_map/ppermute | solution.py:22
  167.3 2.0 collective-permute-start.12
  170.5 8.3 %collective-permute-done.12 = bf16[128,768]{1,0:T(8,128)(2,1)S(1)} collective-permute-done((bf16[128,768]{1,0:T(8,128)(2,1)}, bf16[128,768]{1,0:T(8,128)(2,1)S(1)}, u32[]{:S(2)}, u32[]{:S(2)}) %collective-permute-start.12) | collective-permute-done | bytes 196640 | tf_op jit(solution)/shard_map/ppermute | solution.py:22
  178.8 1.9 collective-permute-start.13
  180.8 1.6 constant_dynamic-update-slice_fusion.16
  182.4 7.6 %collective-permute-done.13 = bf16[128,768]{1,0:T(8,128)(2,1)S(1)} collective-permute-done((bf16[128,768]{1,0:T(8,128)(2,1)S(1)}, bf16[128,768]{1,0:T(8,128)(2,1)S(1)}, u32[]{:S(2)}, u32[]{:S(2)}) %collective-permute-start.13) | collective-permute-done | bytes 196640 | tf_op jit(solution)/shard_map/ppermute | solution.py:22
  190.0 1.9 collective-permute-start.14
  191.9 1.6 constant_dynamic-update-slice_fusion.15
  193.5 1.6 constant_dynamic-update-slice_fusion.14
  195.1 6.1 %collective-permute-done.14 = bf16[128,768]{1,0:T(8,128)(2,1)S(1)} collective-permute-done((bf16[128,768]{1,0:T(8,128)(2,1)S(1)}, bf16[128,768]{1,0:T(8,128)(2,1)S(1)}, u32[]{:S(2)}, u32[]{:S(2)}) %collective-permute-start.14) | collective-permute-done | bytes 196640 | tf_op jit(solution)/shard_map/ppermute | solution.py:22
  201.2 1.9 collective-permute-start.15
  203.8 1.6 constant_dynamic-update-slice_fusion.12
  205.5 6.9 %collective-permute-done.15 = bf16[128,768]{1,0:T(8,128)(2,1)S(1)} collective-permute-done((bf16[128,768]{1,0:T(8,128)(2,1)S(1)}, bf16[128,768]{1,0:T(8,128)(2,1)S(1)}, u32[]{:S(2)}, u32[]{:S(2)}) %collective-permute-start.15) | collective-permute-done | bytes 196640 | tf_op jit(solution)/shard_map/ppermute | solution.py:22
  212.4 1.9 collective-permute-start.16
  215.7 7.9 %collective-permute-done.16 = bf16[128,768]{1,0:T(8,128)(2,1)S(1)} collective-permute-done((bf16[128,768]{1,0:T(8,128)(2,1)S(1)}, bf16[128,768]{1,0:T(8,128)(2,1)S(1)}, u32[]{:S(2)}, u32[]{:S(2)}) %collective-permute-start.16) | collective-permute-done | bytes 196640 | tf_op jit(solution)/shard_map/ppermute | solution.py:22
  223.6 1.9 collective-permute-start.17
  226.9 7.9 %collective-permute-done.17 = bf16[128,768]{1,0:T(8,128)(2,1)S(1)} collective-permute-done((bf16[128,768]{1,0:T(8,128)(2,1)S(1)}, bf16[128,768]{1,0:T(8,128)(2,1)S(1)}, u32[]{:S(2)}, u32[]{:S(2)}) %collective-permute-start.17) | collective-permute-done | bytes 196640 | tf_op jit(solution)/shard_map/ppermute | solution.py:22
  234.8 1.9 collective-permute-start.18
  238.1 7.9 %collective-permute-done.18 = bf16[128,768]{1,0:T(8,128)(2,1)S(1)} collective-permute-done((bf16[128,768]{1,0:T(8,128)(2,1)S(1)}, bf16[128,768]{1,0:T(8,128)(2,1)S(1)}, u32[]{:S(2)}, u32[]{:S(2)}) %collective-permute-start.18) | collective-permute-done | bytes 196640 | tf_op jit(solution)/shard_map/ppermute | solution.py:22
  246.7 3.5 %fusion.42 = (bf16[1664,384]{1,0:T(8,128)(2,1)}, bf16[1664,384]{1,0:T(8,128)(2,1)}) fusion(bf16[1664,768]{1,0:T(8,128)(2,1)} %constant_dynamic-update-slice_fusion.5), kind=kLoop, calls=%fused_computation.109 | loop fusion | bytes 5111808 | tf_op jit(solution)/shard_map/slice | solution.py:210
  250.1 2.5 copy.51
  252.7 2.5 copy.50
  255.2 9.0 %fusion.2 = (f32[6,3,128]{2,1,0:T(4,128)S(1)}, f32[6,1664,128,3]{2,1,3,0:T(8,128)}) fusion(pred[128,1664]{0,1:T(8,128)(4,1)S(1)} %compare_and_fusion, bf16[1664,6,64,1]{0,2,3,1:T(8,128)(2,1)} %bitcast.101, bf16[128,6,3,64]{0,3,2,1:T(8,128)(2,1)S(1)} %bitcast.105), kind=kOutput, calls=%fused_computation.7 | convolution fusion | flops 502232832 | bytes 17130496 | tf_op jit(solution)/shard_map/qkzr,ckr->kzqc/dot_general | solution.py:212
  264.2 8.6 %fusion = f32[6,3,128]{2,1,0:T(4,128)S(1)} fusion(f32[6,1664,128,3]{2,1,3,0:T(8,128)} %get-tuple-element.17, f32[6,3,128]{2,1,0:T(4,128)S(1)} %get-tuple-element.16, pred[128,1664]{0,1:T(8,128)(4,1)S(1)} %compare_and_fusion), kind=kLoop, calls=%fused_computation.5 | loop fusion | flops 15333120 | bytes 15566848 | tf_op jit(solution)/shard_map/reduce_sum | solution.py:218
  272.8 9.2 %fusion.23 = bf16[128,6,3,64]{0,3,2,1:T(8,128)(2,1)S(1)} fusion(bf16[1664,6,64,1]{0,2,3,1:T(8,128)(2,1)S(1)} %bitcast.109, f32[6,1664,128,3]{2,1,3,0:T(8,128)} %get-tuple-element.17, f32[6,3,128]{2,1,0:T(4,128)S(1)} %get-tuple-element.16, pred[128,1664]{0,1:T(8,128)(4,1)S(1)} %compare_and_fusion, f32[128,6,3]{0,2,1:T(4,128)S(1)} %bitcast.116), kind=kOutput, calls=%fused_computation.34 | convolution fusion | flops 506363904 | bytes 17139712 | tf_op jit(solution)/shard_map/iyxv,vip->xiyp/dot_general | solution.py:220
  282.5 1.3 fusion.7
  (157 shorter events, 39.3 us)
Async XLA Ops:
  0.6 157.3 %copy-start = (bf16[1152,1152]{1,0:T(8,128)(2,1)S(1)}, bf16[1152,1152]{1,0:T(8,128)(2,1)}, u32[]{:S(2)}) copy-start(bf16[1152,1152]{1,0:T(8,128)(2,1)} %param.18) | copy-start | bytes 7962628
  0.6 10.5 %copy-start.1 = (s32[64]{0:T(128)S(1)}, s32[64]{0:T(128)}, u32[]{:S(2)}) copy-start(s32[64]{0:T(128)} %param.28) | copy-start | bytes 772
  5.6 11.0 %collective-permute-start.1 = (bf16[8,7680]{1,0:T(8,128)(2,1)S(1)}, bf16[8,7680]{1,0:T(8,128)(2,1)S(1)}, u32[]{:S(2)}, u32[]{:S(2)}) collective-permute-start(bf16[8,7680]{1,0:T(8,128)(2,1)S(1)} %constant_dynamic-update-slice_fusion), channel_id=1, source_target_pairs={{0,7},{1,0},{2,1},{3,2},{4,3},{5,4},{6,5},{7,6},{8,15},{9,8},{10,9... | collective-permute-start | bytes 368648 | tf_op jit(solution)/shard_map/ppermute | solution.py:138
  7.8 11.8 %collective-permute-start = (bf16[8,7680]{1,0:T(8,128)(2,1)S(1)}, bf16[8,7680]{1,0:T(8,128)(2,1)S(1)}, u32[]{:S(2)}, u32[]{:S(2)}) collective-permute-start(bf16[8,7680]{1,0:T(8,128)(2,1)S(1)} %constant_dynamic-update-slice_fusion), channel_id=1, source_target_pairs={{0,1},{1,2},{2,3},{3,4},{4,5},{5,6},{6,7},{7,0},{8,9},{9,10},{10,1... | collective-permute-start | bytes 368648 | tf_op jit(solution)/shard_map/ppermute | solution.py:133
  7.8 3.2 %copy-start.26 = (s32[128]{0:T(128)}, s32[128]{0:T(128)S(1)}, u32[]{:S(2)}) copy-start(s32[128]{0:T(128)S(1)} %iota_add_fusion.1) | copy-start | bytes 1540
  8.9 7.0 %copy-start.17 = (s32[1664]{0:T(1024)}, s32[1664]{0:T(1024)S(1)}, u32[]{:S(2)}) copy-start(s32[1664]{0:T(1024)S(1)} %iota_add_fusion) | copy-start | bytes 19972
  10.8 44.9 %copy-start.28 = (s32[128]{0:T(128)}, s32[128]{0:T(128)S(1)}, u32[]{:S(2)}) copy-start(s32[128]{0:T(128)S(1)} %broadcast_add_fusion.1) | copy-start | bytes 1540
  11.1 1.5 copy-start.2
  16.6 5.4 %collective-permute-start.3 = (bf16[8,7680]{1,0:T(8,128)(2,1)S(1)}, bf16[8,7680]{1,0:T(8,128)(2,1)S(1)}, u32[]{:S(2)}, u32[]{:S(2)}) collective-permute-start(bf16[8,7680]{1,0:T(8,128)(2,1)S(1)} %collective-permute-done.1), channel_id=1, source_target_pairs={{0,7},{1,0},{2,1},{3,2},{4,3},{5,4},{6,5},{7,6},{8,15},{9,8},{10,9... | collective-permute-start | bytes 368648 | tf_op jit(solution)/shard_map/ppermute | solution.py:138
  19.5 5.5 %collective-permute-start.2 = (bf16[8,7680]{1,0:T(8,128)(2,1)S(1)}, bf16[8,7680]{1,0:T(8,128)(2,1)S(1)}, u32[]{:S(2)}, u32[]{:S(2)}) collective-permute-start(bf16[8,7680]{1,0:T(8,128)(2,1)S(1)} %collective-permute-done), channel_id=1, source_target_pairs={{0,1},{1,2},{2,3},{3,4},{4,5},{5,6},{6,7},{7,0},{8,9},{9,10},{10,1... | collective-permute-start | bytes 368648 | tf_op jit(solution)/shard_map/ppermute | solution.py:133
  22.0 9.2 %collective-permute-start.5 = (bf16[8,7680]{1,0:T(8,128)(2,1)S(1)}, bf16[8,7680]{1,0:T(8,128)(2,1)S(1)}, u32[]{:S(2)}, u32[]{:S(2)}) collective-permute-start(bf16[8,7680]{1,0:T(8,128)(2,1)S(1)} %collective-permute-done.3), channel_id=1, source_target_pairs={{0,7},{1,0},{2,1},{3,2},{4,3},{5,4},{6,5},{7,6},{8,15},{9,8},{10,9... | collective-permute-start | bytes 368648 | tf_op jit(solution)/shard_map/ppermute | solution.py:138
  25.0 5.5 %collective-permute-start.4 = (bf16[8,7680]{1,0:T(8,128)(2,1)S(1)}, bf16[8,7680]{1,0:T(8,128)(2,1)S(1)}, u32[]{:S(2)}, u32[]{:S(2)}) collective-permute-start(bf16[8,7680]{1,0:T(8,128)(2,1)S(1)} %collective-permute-done.2), channel_id=1, source_target_pairs={{0,1},{1,2},{2,3},{3,4},{4,5},{5,6},{6,7},{7,0},{8,9},{9,10},{10,1... | collective-permute-start | bytes 368648 | tf_op jit(solution)/shard_map/ppermute | solution.py:133
  30.6 5.5 %collective-permute-start.6 = (bf16[8,7680]{1,0:T(8,128)(2,1)S(1)}, bf16[8,7680]{1,0:T(8,128)(2,1)S(1)}, u32[]{:S(2)}, u32[]{:S(2)}) collective-permute-start(bf16[8,7680]{1,0:T(8,128)(2,1)S(1)} %collective-permute-done.4), channel_id=1, source_target_pairs={{0,1},{1,2},{2,3},{3,4},{4,5},{5,6},{6,7},{7,0},{8,9},{9,10},{10,1... | collective-permute-start | bytes 368648 | tf_op jit(solution)/shard_map/ppermute | solution.py:133
  47.3 8.3 %copy-start.23 = (bf16[1152]{0:T(1024)(128)(2,1)S(1)}, bf16[1152]{0:T(1024)(128)(2,1)}, u32[]{:S(2)}) copy-start(bf16[1152]{0:T(1024)(128)(2,1)} %param.17) | copy-start | bytes 6916
  47.3 30.4 %all-to-all-start = ((bf16[16,5,7680]{2,1,0:T(8,128)(2,1)}), bf16[16,5,7680]{2,1,0:T(8,128)(2,1)}, u32[]{:S(2)}, u32[]{:S(2)}) async-start(bf16[16,5,7680]{2,1,0:T(8,128)(2,1)} %broadcast_select_fusion), calls=%async_computation | async-start | bytes 3932160 | tf_op jit(solution)/shard_map/all_to_all | solution.py:159
  55.7 36.1 %copy-start.15 = (f32[1152]{0:T(1024)}, f32[1152]{0:T(1024)S(1)}, u32[]{:S(2)}) copy-start(f32[1152]{0:T(1024)S(1)} %convert_element_type.91) | copy-start | bytes 13828
  55.7 36.1 %copy-start.21 = (f32[128]{0:T(128)}, f32[128]{0:T(128)S(1)}, u32[]{:S(2)}) copy-start(f32[128]{0:T(128)S(1)} %add_rsqrt_fusion) | copy-start | bytes 1540
  55.8 36.0 %copy-start.24 = (f32[128,5]{0,1:T(8,128)}, f32[128,5]{0,1:T(8,128)S(1)}, u32[]{:S(2)}) copy-start(f32[128,5]{0,1:T(8,128)S(1)} %fusion.34) | copy-start | bytes 7684
  56.5 39.6 %copy-start.12 = (f32[128,32]{0,1:T(8,128)}, f32[128,32]{0,1:T(8,128)S(1)}, u32[]{:S(2)}) copy-start(f32[128,32]{0,1:T(8,128)S(1)} %get-tuple-element.14) | copy-start | bytes 49156
  84.4 7.3 %copy-start.3 = (bf16[128,1152]{1,0:T(8,128)(2,1)S(1)}, bf16[128,1152]{1,0:T(8,128)(2,1)}, u32[]{:S(2)}) copy-start(bf16[128,1152]{1,0:T(8,128)(2,1)} %param.16) | copy-start | bytes 884740
  92.2 2.1 copy-start.19
  96.0 4.5 %copy-start.20 = (s32[1664]{0:T(1024)S(1)}, s32[1664]{0:T(1024)}, u32[]{:S(2)}) copy-start(s32[1664]{0:T(1024)} %convert_reduce_fusion) | copy-start | bytes 19972
  96.1 15.7 %copy-start.18 = (s32[1664]{0:T(1024)S(1)}, s32[1664]{0:T(1024)}, u32[]{:S(2)}) copy-start(s32[1664]{0:T(1024)} %copy-done.17) | copy-start | bytes 19972
  96.1 15.7 %copy-start.27 = (s32[128]{0:T(128)S(1)}, s32[128]{0:T(128)}, u32[]{:S(2)}) copy-start(s32[128]{0:T(128)} %copy-done.26) | copy-start | bytes 1540
  96.1 15.7 %copy-start.29 = (s32[128]{0:T(128)S(1)}, s32[128]{0:T(128)}, u32[]{:S(2)}) copy-start(s32[128]{0:T(128)} %copy-done.28) | copy-start | bytes 1540
  98.6 29.6 %copy-start.6 = (bf16[128,768]{1,0:T(8,128)(2,1)}, bf16[128,768]{1,0:T(8,128)(2,1)S(1)}, u32[]{:S(2)}) copy-start(bf16[128,768]{1,0:T(8,128)(2,1)S(1)} %pad_maximum_fusion.1) | copy-start | bytes 589828
  98.6 11.2 %collective-permute-start.7 = (bf16[128,768]{1,0:T(8,128)(2,1)S(1)}, bf16[128,768]{1,0:T(8,128)(2,1)S(1)}, u32[]{:S(2)}, u32[]{:S(2)}) collective-permute-start(bf16[128,768]{1,0:T(8,128)(2,1)S(1)} %pad_maximum_fusion.1), channel_id=1, source_target_pairs={{0,1},{1,2},{2,3},{3,4},{4,5},{5,6},{6,7},{7,8},{8,9},{9,10},{10,1... | collective-permute-start | bytes 589832 | tf_op jit(solution)/shard_map/ppermute | solution.py:22
  109.8 11.3 %copy-start.8 = (bf16[128,768]{1,0:T(8,128)(2,1)}, bf16[128,768]{1,0:T(8,128)(2,1)S(1)}, u32[]{:S(2)}) copy-start(bf16[128,768]{1,0:T(8,128)(2,1)S(1)} %collective-permute-done.7) | copy-start | bytes 589828
  109.8 11.3 %collective-permute-start.8 = (bf16[128,768]{1,0:T(8,128)(2,1)S(1)}, bf16[128,768]{1,0:T(8,128)(2,1)}, u32[]{:S(2)}, u32[]{:S(2)}) collective-permute-start(bf16[128,768]{1,0:T(8,128)(2,1)S(1)} %collective-permute-done.7), channel_id=1, source_target_pairs={{0,1},{1,2},{2,3},{3,4},{4,5},{5,6},{6,7},{7,8},{8,9},{9,10},{10,1... | collective-permute-start | bytes 589832 | tf_op jit(solution)/shard_map/ppermute | solution.py:22
  121.1 23.4 %collective-permute-start.9 = (bf16[128,768]{1,0:T(8,128)(2,1)}, bf16[128,768]{1,0:T(8,128)(2,1)}, u32[]{:S(2)}, u32[]{:S(2)}) collective-permute-start(bf16[128,768]{1,0:T(8,128)(2,1)} %collective-permute-done.8), channel_id=1, source_target_pairs={{0,1},{1,2},{2,3},{3,4},{4,5},{5,6},{6,7},{7,8},{8,9},{9,10},{10,1... | collective-permute-start | bytes 589832 | tf_op jit(solution)/shard_map/ppermute | solution.py:22
  133.3 24.6 %copy-start.16 = (f32[1152]{0:T(1024)S(1)}, f32[1152]{0:T(1024)}, u32[]{:S(2)}) copy-start(f32[1152]{0:T(1024)} %copy-done.15) | copy-start | bytes 13828
  133.3 24.7 %copy-start.22 = (f32[128]{0:T(128)S(1)}, f32[128]{0:T(128)}, u32[]{:S(2)}) copy-start(f32[128]{0:T(128)} %copy-done.21) | copy-start | bytes 1540
  144.5 11.4 %collective-permute-start.10 = (bf16[128,768]{1,0:T(8,128)(2,1)}, bf16[128,768]{1,0:T(8,128)(2,1)S(1)}, u32[]{:S(2)}, u32[]{:S(2)}) collective-permute-start(bf16[128,768]{1,0:T(8,128)(2,1)} %collective-permute-done.9), channel_id=1, source_target_pairs={{0,1},{1,2},{2,3},{3,4},{4,5},{5,6},{6,7},{7,8},{8,9},{9,10},{10,1... | collective-permute-start | bytes 589832 | tf_op jit(solution)/shard_map/ppermute | solution.py:22
  147.5 21.9 %copy-start.13 = (f32[128,32]{0,1:T(8,128)S(1)}, f32[128,32]{0,1:T(8,128)}, u32[]{:S(2)}) copy-start(f32[128,32]{0,1:T(8,128)} %copy-done.12) | copy-start | bytes 49156
  147.5 21.9 %copy-start.14 = (f32[128,32]{0,1:T(8,128)S(1)}, f32[128,32]{0,1:T(8,128)}, u32[]{:S(2)}) copy-start(f32[128,32]{0,1:T(8,128)} %get-tuple-element.15) | copy-start | bytes 49156
  156.0 5.5 %copy-start.9 = (bf16[128,768]{1,0:T(8,128)(2,1)}, bf16[128,768]{1,0:T(8,128)(2,1)S(1)}, u32[]{:S(2)}) copy-start(bf16[128,768]{1,0:T(8,128)(2,1)S(1)} %collective-permute-done.10) | copy-start | bytes 589828
  156.0 11.3 %collective-permute-start.11 = (bf16[128,768]{1,0:T(8,128)(2,1)S(1)}, bf16[128,768]{1,0:T(8,128)(2,1)}, u32[]{:S(2)}, u32[]{:S(2)}) collective-permute-start(bf16[128,768]{1,0:T(8,128)(2,1)S(1)} %collective-permute-done.10), channel_id=1, source_target_pairs={{0,1},{1,2},{2,3},{3,4},{4,5},{5,6},{6,7},{7,8},{8,9},{9,10},{10,1... | collective-permute-start | bytes 589832 | tf_op jit(solution)/shard_map/ppermute | solution.py:22
  167.3 35.9 %copy-start.10 = (bf16[128,768]{1,0:T(8,128)(2,1)S(1)}, bf16[128,768]{1,0:T(8,128)(2,1)}, u32[]{:S(2)}) copy-start(bf16[128,768]{1,0:T(8,128)(2,1)} %copy-done.9) | copy-start | bytes 589828
  167.3 11.5 %collective-permute-start.12 = (bf16[128,768]{1,0:T(8,128)(2,1)}, bf16[128,768]{1,0:T(8,128)(2,1)S(1)}, u32[]{:S(2)}, u32[]{:S(2)}) collective-permute-start(bf16[128,768]{1,0:T(8,128)(2,1)} %collective-permute-done.11), channel_id=1, source_target_pairs={{0,1},{1,2},{2,3},{3,4},{4,5},{5,6},{6,7},{7,8},{8,9},{9,10},{10,1... | collective-permute-start | bytes 589832 | tf_op jit(solution)/shard_map/ppermute | solution.py:22
  178.8 11.2 %collective-permute-start.13 = (bf16[128,768]{1,0:T(8,128)(2,1)S(1)}, bf16[128,768]{1,0:T(8,128)(2,1)S(1)}, u32[]{:S(2)}, u32[]{:S(2)}) collective-permute-start(bf16[128,768]{1,0:T(8,128)(2,1)S(1)} %collective-permute-done.12), channel_id=1, source_target_pairs={{0,1},{1,2},{2,3},{3,4},{4,5},{5,6},{6,7},{7,8},{8,9},{9,10},{10,1... | collective-permute-start | bytes 589832 | tf_op jit(solution)/shard_map/ppermute | solution.py:22
  190.0 11.2 %collective-permute-start.14 = (bf16[128,768]{1,0:T(8,128)(2,1)S(1)}, bf16[128,768]{1,0:T(8,128)(2,1)S(1)}, u32[]{:S(2)}, u32[]{:S(2)}) collective-permute-start(bf16[128,768]{1,0:T(8,128)(2,1)S(1)} %collective-permute-done.13), channel_id=1, source_target_pairs={{0,1},{1,2},{2,3},{3,4},{4,5},{5,6},{6,7},{7,8},{8,9},{9,10},{10,1... | collective-permute-start | bytes 589832 | tf_op jit(solution)/shard_map/ppermute | solution.py:22
  201.2 11.2 %collective-permute-start.15 = (bf16[128,768]{1,0:T(8,128)(2,1)S(1)}, bf16[128,768]{1,0:T(8,128)(2,1)S(1)}, u32[]{:S(2)}, u32[]{:S(2)}) collective-permute-start(bf16[128,768]{1,0:T(8,128)(2,1)S(1)} %collective-permute-done.14), channel_id=1, source_target_pairs={{0,1},{1,2},{2,3},{3,4},{4,5},{5,6},{6,7},{7,8},{8,9},{9,10},{10,1... | collective-permute-start | bytes 589832 | tf_op jit(solution)/shard_map/ppermute | solution.py:22
  212.4 11.2 %collective-permute-start.16 = (bf16[128,768]{1,0:T(8,128)(2,1)S(1)}, bf16[128,768]{1,0:T(8,128)(2,1)S(1)}, u32[]{:S(2)}, u32[]{:S(2)}) collective-permute-start(bf16[128,768]{1,0:T(8,128)(2,1)S(1)} %collective-permute-done.15), channel_id=1, source_target_pairs={{0,1},{1,2},{2,3},{3,4},{4,5},{5,6},{6,7},{7,8},{8,9},{9,10},{10,1... | collective-permute-start | bytes 589832 | tf_op jit(solution)/shard_map/ppermute | solution.py:22
  223.6 11.2 %collective-permute-start.17 = (bf16[128,768]{1,0:T(8,128)(2,1)S(1)}, bf16[128,768]{1,0:T(8,128)(2,1)S(1)}, u32[]{:S(2)}, u32[]{:S(2)}) collective-permute-start(bf16[128,768]{1,0:T(8,128)(2,1)S(1)} %collective-permute-done.16), channel_id=1, source_target_pairs={{0,1},{1,2},{2,3},{3,4},{4,5},{5,6},{6,7},{7,8},{8,9},{9,10},{10,1... | collective-permute-start | bytes 589832 | tf_op jit(solution)/shard_map/ppermute | solution.py:22
  234.8 11.2 %collective-permute-start.18 = (bf16[128,768]{1,0:T(8,128)(2,1)S(1)}, bf16[128,768]{1,0:T(8,128)(2,1)S(1)}, u32[]{:S(2)}, u32[]{:S(2)}) collective-permute-start(bf16[128,768]{1,0:T(8,128)(2,1)S(1)} %collective-permute-done.17), channel_id=1, source_target_pairs={{0,1},{1,2},{2,3},{3,4},{4,5},{5,6},{6,7},{7,8},{8,9},{9,10},{10,1... | collective-permute-start | bytes 589832 | tf_op jit(solution)/shard_map/ppermute | solution.py:22
  264.2 8.6 %copy-start.5 = (bf16[1664,384]{0,1:T(8,128)(2,1)S(1)}, bf16[1664,384]{0,1:T(8,128)(2,1)}, u32[]{:S(2)}) copy-start(bf16[1664,384]{0,1:T(8,128)(2,1)} %copy.50) | copy-start | bytes 3833860
  272.8 9.3 %copy-start.11 = (bf16[5,16,1152]{2,1,0:T(8,128)(2,1)S(1)}, bf16[5,16,1152]{2,1,0:T(8,128)(2,1)}, u32[]{:S(2)}) copy-start(bf16[5,16,1152]{2,1,0:T(8,128)(2,1)} %dot_general.51) | copy-start | bytes 552964
  272.8 9.3 %copy-start.25 = (f32[128,5]{0,1:T(8,128)S(1)}, f32[128,5]{0,1:T(8,128)}, u32[]{:S(2)}) copy-start(f32[128,5]{0,1:T(8,128)} %copy-done.24) | copy-start | bytes 7684
  272.8 9.5 %copy-start.7 = (bf16[80,1152]{1,0:T(8,128)(2,1)S(1)}, bf16[80,1152]{1,0:T(8,128)(2,1)}, u32[]{:S(2)}) copy-start(bf16[80,1152]{1,0:T(8,128)(2,1)} %reshape_reshape.9) | copy-start | bytes 552964
  272.8 9.7 %copy-start.4 = (bf16[1152,1152]{1,0:T(8,128)(2,1)S(1)}, bf16[1152,1152]{1,0:T(8,128)(2,1)}, u32[]{:S(2)}) copy-start(bf16[1152,1152]{1,0:T(8,128)(2,1)} %param.21) | copy-start | bytes 7962628
